TPU v7x, 32 devices: a whole 2x2x4 slice. The times are simulated.
32 devices in a mesh: dp: 4 (over z), space: 4 (over x, core), rep: 2 (over y).
Axes of the slice: x: 2, y: 2, z: 4, core: 2. Of those that a mesh axis runs over, the one named last changes fastest.
Arguments:
- frames: bfloat16 [6, 8, 32, 32, 512], P(None, ('dp', 'rep'), 'space'), may hold values from -6 to 6
- membrane: bfloat16 [8, 32, 32, 512], P(('dp', 'rep'), 'space'), may hold values from -6 to 6
- cotangent: bfloat16 [6, 8, 32, 32, 512], P(None, ('dp', 'rep'), 'space'), may hold values from -6 to 6
- master: float32 [4608, 512], P('dp'), may hold values from -0.09375 to 0.09375
- moment: float32 [4608, 512], P('dp'), may hold values from -4 to 4
- second: float32 [4608, 512], P('dp'), may hold values from 0.05 to 5
Outputs:
- grad_input: bfloat16 [6, 8, 32, 32, 512], P(None, ('dp', 'rep'), 'space')
- membrane_grad: float32 [8, 32, 32, 512], P(('dp', 'rep'), 'space')
- weight_grad: float32 [4608, 512], P('dp')
- new_moment: float32 [4608, 512], P('dp')
- new_second: float32 [4608, 512], P('dp')
- update: float32 [4608, 512], P('dp')
All inputs are finite; a program needn't handle non-finite values.
Results may differ from a plain program's by a relative error of at most 0.003.
Values may be sent and summed in bfloat16 or wider, within the bound.
No kernel may reach another device: no remote copies, remote signals or barrier semaphores. Data moves between devices by JAX's collectives and lax.ppermute only.
A program may use at most 192 MiB of HBM per device.

v0:
```python
import math
import jax
import jax.numpy as jnp
from jax import lax
from jax.sharding import PartitionSpec as P


def extended(x, sides, width):
    for axis, dim in sides:
        peers, length = (lax.axis_size(axis), x.shape[dim])
        up = [(i, (i + 1) % peers) for i in range(peers - 1)]
        down = [(j, i) for i, j in up]
        last = lax.slice_in_dim(x, length - width, length, axis=dim)
        first = lax.slice_in_dim(x, 0, width, axis=dim)
        before = lax.ppermute(last, axis, up)
        after = lax.ppermute(first, axis, down)
        x = jnp.concatenate([before, x, after], axis=dim)
    return x


def surrogate(potential):
    return 1.0 / (1.0 + (math.pi * (potential - 1.0)) ** 2)


def offsets_list():
    return [(row_shift, col_shift) for row_shift in (-1, 0, 1) for col_shift in (-1, 0, 1)]


def on_device(frames, membrane, cotangent, master, moment, second):
    steps_count, samples, rows, cols, chans = frames.shape
    weights = lax.all_gather(master.astype(jnp.bfloat16), "dp", axis=0, tiled=True)
    stacked = jnp.concatenate([membrane[None], frames], axis=0)
    rimmed = extended(stacked, (("space", 2),), 1)
    voltage = rimmed[0].astype(jnp.float32)
    potentials = []
    fired = []
    for position in range(steps_count):
        potential = 0.5 * voltage + rimmed[position + 1].astype(jnp.float32)
        spikes = jnp.where(potential >= 1.0, jnp.float32(1.0), jnp.float32(0.0))
        voltage = potential - spikes
        potentials.append(potential[:, 1:-1])
        fired.append(spikes)
    potential_all = jnp.stack(potentials)
    spike_all = jnp.stack(fired).astype(jnp.bfloat16)
    col_pad = ((0, 0), (0, 0), (0, 0), (1, 1), (0, 0))
    spike_pad = jnp.pad(spike_all, col_pad)
    grad_rim = extended(cotangent, (("space", 2),), 1)
    grad_pad = jnp.pad(grad_rim, col_pad)
    spike_cols = jnp.concatenate(
        [spike_pad[:, :, 1 + a : 1 + a + rows, 1 + b : 1 + b + cols] for a, b in offsets_list()],
        axis=-1,
    ).reshape(-1, 9 * chans)
    grad_cols = jnp.concatenate(
        [grad_pad[:, :, 1 - a : 1 - a + rows, 1 - b : 1 - b + cols] for a, b in offsets_list()],
        axis=-1,
    ).reshape(-1, 9, chans)
    grad_flat = cotangent.reshape(-1, chans)
    weight_local = lax.dot_general(
        spike_cols, grad_flat, (((0,), (0,)), ((), ())), preferred_element_type=jnp.float32
    )
    dspikes = jnp.einsum(
        "nkd,kcd->nc",
        grad_cols,
        weights.reshape(9, chans, chans),
        preferred_element_type=jnp.float32,
    )
    dspikes = dspikes.reshape(steps_count, samples, rows, cols, chans)
    carried = jnp.zeros((samples, rows, cols, chans), jnp.float32)
    outs = [None] * steps_count
    for position in reversed(range(steps_count)):
        carried = dspikes[position] * surrogate(potential_all[position]) + 0.5 * carried
        outs[position] = (cotangent[position].astype(jnp.float32) + carried).astype(jnp.bfloat16)
    grad_input = jnp.stack(outs)
    membrane_grad = 0.5 * carried
    data_count = lax.axis_size("dp")
    total_cells = samples * data_count * lax.axis_size("rep") * rows * lax.axis_size("space") * cols
    shard_part = lax.psum_scatter(weight_local, "dp", scatter_dimension=0, tiled=True)
    summed = lax.psum(shard_part, ("space", "rep"))
    weight_grad = summed * (1.0 / math.sqrt(steps_count * total_cells))
    new_moment = 0.9 * moment + 0.1 * weight_grad
    new_second = 0.95 * second + 0.05 * weight_grad * weight_grad
    update = new_moment / (jnp.sqrt(new_second) + 1e-08)
    return (grad_input, membrane_grad, weight_grad, new_moment, new_second, update)


def solution(mesh):
    return jax.shard_map(
        on_device,
        mesh=mesh,
        in_specs=(
            P(None, ("dp", "rep"), "space", None, None),
            P(("dp", "rep"), "space", None, None),
            P(None, ("dp", "rep"), "space", None, None),
            P("dp", None),
            P("dp", None),
            P("dp", None),
        ),
        out_specs=(
            P(None, ("dp", "rep"), "space", None, None),
            P(("dp", "rep"), "space", None, None),
            P("dp", None),
            P("dp", None),
            P("dp", None),
            P("dp", None),
        ),
        check_vma=False,
    )
```

profile of v0, /device:TPU:0, one launch (start us, length us, event | category | flops | bytes accessed | tf_op | source)
XLA Modules:
  0.0 351.5 jit_solution(18133478292274602957)
XLA Ops:
  7.2 1.1 pad_maximum_fusion.4
  8.3 1.3 collective-permute-start.3
  9.6 3.2 collective-permute-start.2
  12.8 2.8 convert_element_type.357
  15.7 1.8 pad_maximum_fusion
  24.6 10.2 %fusion.4 = f32[4608,512]{1,0:T(8,128)} fusion(bf16[6,1,8,32,4608]{4,3,2,0,1:T(8,128)(2,1)S(1)} %fusion.21, bf16[6,1,8,32,512]{4,3,2,1,0:T(8,128)(2,1)S(1)} %copy-done), kind=kOutput, calls=%fused_computation.4 | convolution fusion | flops 7247757312 | bytes 25165824 | tf_op jit(solution)/shard_map/dot_general | solution.py:58
  34.8 1.1 fusion.104
  35.9 1.3 collective-permute-start.1
  37.2 5.5 %collective-permute-start = (bf16[6,1,1,32,512]{4,3,2,1,0:T(8,128)(2,1)S(1)}, bf16[6,1,1,32,512]{4,3,2,1,0:T(8,128)(2,1)S(1)}, u32[]{:S(2)}, u32[]{:S(2)}) collective-permute-start(bf16[6,1,1,32,512]{4,3,2,1,0:T(8,128)(2,1)S(1)} %get-tuple-element.29), channel_id=1, source_target_pairs={{0,2},{2,4},{4,6},{1,3},{3,5},{5,7},{8,10},{10,12},{12,14},{9,11},... | collective-permute-start | bytes 589832 | tf_op jit(solution)/shard_map/ppermute | solution.py:15
  42.7 0.8 collective-permute-done
  43.5 2.3 fusion.15
  45.9 1.7 slice_dynamic-update-slice_fusion.8
  47.5 1.4 fusion.23
  49.0 1.4 slice_dynamic-update-slice_fusion.7
  50.4 2.1 slice_dynamic-update-slice_fusion.6
  52.5 1.4 constant_dynamic-update-slice_fusion
  53.8 1.4 slice_dynamic-update-slice_fusion.5
  55.2 2.0 slice_dynamic-update-slice_fusion.4
  57.2 1.4 fusion.22
  58.6 1.4 slice_dynamic-update-slice_fusion.3
  60.0 26.6 %reshape.515 = bf16[1536,9,512]{2,1,0:T(8,128)(2,1)} reshape(bf16[6,1,8,32,4608]{4,3,2,1,0:T(8,128)(2,1)} %slice_dynamic-update-slice_fusion.3) | data formatting | bytes 28311552 | tf_op jit(solution)/shard_map/reshape | solution.py:56
  86.6 1.0 fusion.73
  87.6 0.9 convert_bitcast_fusion.1
  88.6 1.8 fusion.28
  90.4 17.5 %all-gather.2.cloned.1.call-done = bf16[4608,512]{1,0:T(8,128)(2,1)} async-done(((bf16[1152,512]{1,0:T(8,128)(2,1)}), bf16[4608,512]{1,0:T(8,128)(2,1)}) %all-gather.2.cloned.1.call-update) | async-done | bytes 4718608 | tf_op jit(solution)/shard_map/all_gather | solution.py:31
  107.9 25.8 %fusion.8 = f32[1536,512]{1,0:T(8,128)S(1)} fusion(bf16[9,512,512]{2,1,0:T(8,128)(2,1)} %bitcast.158, bf16[1536,9,512]{2,1,0:T(8,128)(2,1)} %reshape.515), kind=kOutput, calls=%fused_computation.8 | convolution fusion | flops 7247757312 | bytes 22020096 | tf_op jit(solution)/shard_map/nkd,kcd->nc/dot_general | solution.py:61
  135.8 1.7 broadcast_multiply_fusion.1
  138.3 131.7 %reduce-scatter.2.cloned.1.call-done = f32[1152,512]{1,0:T(8,128)} async-done(((f32[4608,512]{1,0:T(8,128)}), f32[1152,512]{1,0:T(8,128)}) %reduce-scatter.2.cloned.1.call-update) | async-done | bytes 2359312 | tf_op jit(solution)/shard_map/reduce_scatter | solution.py:77
  270.1 2.2 fusion.87
  273.9 0.9 fusion.93
  275.6 61.5 %all-reduce.4.cloned.1.call-done = f32[1152,512]{1,0:T(8,128)} async-done(((f32[1152,512]{1,0:T(8,128)}), f32[1152,512]{1,0:T(8,128)}) %all-reduce.4.cloned.1.call-update) | async-done | bytes 2359312 | tf_op jit(solution)/shard_map/psum | solution.py:78
  337.1 7.9 %add_divide_fusion = (f32[1152,512]{1,0:T(8,128)}, f32[1152,512]{1,0:T(8,128)}, f32[1152,512]{1,0:T(8,128)}, f32[1152,512]{1,0:T(8,128)}) fusion(f32[1152,512]{1,0:T(8,128)} %all-reduce.4.cloned.1.call-done, f32[1152,512]{1,0:T(8,128)} %param.11, f32[1152,512]{1,0:T(8,128)} %param.10), kind=kLoop, calls=%fused_computation.14 | loop fusion | flops 5898240 | bytes 16515072 | tf_op jit(solution)/shard_map/div | solution.py:82
  (55 shorter events, 12.3 us)
Async XLA Ops:
  7.2 100.7 %all-gather.2.cloned.1.call-start = ((), (), s32[]{:S(2)}) async-start(), calls=%async_computation.1 | async-start | bytes 5898240 | tf_op jit(solution)/shard_map/all_gather | solution.py:31
  8.3 7.4 %collective-permute-start.3 = (bf16[7,1,1,32,512]{4,3,2,1,0:T(8,128)(2,1)S(1)}, bf16[7,1,1,32,512]{4,3,2,1,0:T(8,128)(2,1)S(1)}, u32[]{:S(2)}, u32[]{:S(2)}) collective-permute-start(bf16[7,1,1,32,512]{4,3,2,1,0:T(8,128)(2,1)S(1)} %get-tuple-element.28), channel_id=1, source_target_pairs={{2,0},{4,2},{6,4},{3,1},{5,3},{7,5},{10,8},{12,10},{14,12},{11,9},... | collective-permute-start | bytes 688136 | tf_op jit(solution)/shard_map/ppermute | solution.py:16
  9.6 6.1 %copy-start.12 = (bf16[1,8,32,512]{3,2,1,0:T(8,128)(2,1)S(1)}, bf16[1,8,32,512]{3,2,1,0:T(8,128)(2,1)}, u32[]{:S(2)}) copy-start(bf16[1,8,32,512]{3,2,1,0:T(8,128)(2,1)} %param.7) | copy-start | bytes 786436
  9.6 6.1 %collective-permute-start.2 = (bf16[7,1,1,32,512]{4,3,2,1,0:T(8,128)(2,1)S(1)}, bf16[7,1,1,32,512]{4,3,2,1,0:T(8,128)(2,1)S(1)}, u32[]{:S(2)}, u32[]{:S(2)}) collective-permute-start(bf16[7,1,1,32,512]{4,3,2,1,0:T(8,128)(2,1)S(1)} %get-tuple-element.27), channel_id=1, source_target_pairs={{0,2},{2,4},{4,6},{1,3},{3,5},{5,7},{8,10},{10,12},{12,14},{9,11},... | collective-permute-start | bytes 688136 | tf_op jit(solution)/shard_map/ppermute | solution.py:15
  15.6 254.4 %reduce-scatter.2.cloned.1.call-start = ((), (), s32[]{:S(2)}) async-start(), calls=%async_computation.2 | async-start | bytes 11796480 | tf_op jit(solution)/shard_map/reduce_scatter | solution.py:77
  23.2 1.4 copy-start
  34.8 302.3 %all-reduce.4.cloned.1.call-start = ((), (), s32[]{:S(2)}) async-start(), calls=%async_computation.3 | async-start | bytes 4718592 | tf_op jit(solution)/shard_map/psum | solution.py:78
  35.9 6.8 %collective-permute-start.1 = (bf16[6,1,1,32,512]{4,3,2,1,0:T(8,128)(2,1)S(1)}, bf16[6,1,1,32,512]{4,3,2,1,0:T(8,128)(2,1)S(1)}, u32[]{:S(2)}, u32[]{:S(2)}) collective-permute-start(bf16[6,1,1,32,512]{4,3,2,1,0:T(8,128)(2,1)S(1)} %get-tuple-element.30), channel_id=1, source_target_pairs={{2,0},{4,2},{6,4},{3,1},{5,3},{7,5},{10,8},{12,10},{14,12},{11,9},... | collective-permute-start | bytes 589832 | tf_op jit(solution)/shard_map/ppermute | solution.py:16
  37.2 6.3 %collective-permute-start = (bf16[6,1,1,32,512]{4,3,2,1,0:T(8,128)(2,1)S(1)}, bf16[6,1,1,32,512]{4,3,2,1,0:T(8,128)(2,1)S(1)}, u32[]{:S(2)}, u32[]{:S(2)}) collective-permute-start(bf16[6,1,1,32,512]{4,3,2,1,0:T(8,128)(2,1)S(1)} %get-tuple-element.29), channel_id=1, source_target_pairs={{0,2},{2,4},{4,6},{1,3},{3,5},{5,7},{8,10},{10,12},{12,14},{9,11},... | collective-permute-start | bytes 589832 | tf_op jit(solution)/shard_map/ppermute | solution.py:15
  45.8 1.7 copy-start.1
  133.7 1.1 copy-start.4
  133.7 1.3 copy-start.6
  133.7 1.5 copy-start.7
  133.8 1.7 copy-start.8
  133.8 1.8 copy-start.9
  133.8 2.0 copy-start.10
  135.8 1.7 copy-start.2
  270.1 2.3 copy-start.3
  270.1 3.0 copy-start.11
  270.1 3.8 %copy-start.5 = (f32[1,10,32,512]{3,2,1,0:T(8,128)S(1)}, f32[1,10,32,512]{3,2,1,0:T(8,128)}, u32[]{:S(2)}) copy-start(f32[1,10,32,512]{3,2,1,0:T(8,128)} %get-tuple-element.17) | copy-start | bytes 1966084
Sparse Core Ops, SparseCore 0:
  15.8 92.1 all-gather.1
  110.3 159.7 reduce-scatter.1
  273.3 63.7 all-reduce.3
where the time goes:
time: 353 us; the launch traced here: 352 us
  waiting for transfers between devices  212 us (60%)
  local copies, waits for them, and re-layouts  46.2 us (13%)
  matrix products  36 us (10%)
  other arithmetic  32.3 us (9%)
  between operations  14.1 us (4%)
  starting transfers between devices  11.3 us (3%)
    reduce_scatter x1, waiting for transfers between devices, on_device(): lax.psum_scatter(weight_local, 'dp', scatter_dimension=0, tiled=True)  132 us
    psum x1, waiting for transfers between devices, on_device(): summed = lax.psum(shard_part, ('space', 'rep'))  61.5 us
    reshape x1, local copies, waits for them, and re-layouts, on_device(): grad_cols = jnp.concatenate([grad_pad[:, :, 1 - a:1 - a + rows, 1 - b:1 -...  26.6 us
    dot_general x1, matrix products, on_device(): jnp.einsum('nkd,kcd->nc', grad_cols, weights.reshape(9, chans, chans), pr...  25.8 us
    all_gather x1, waiting for transfers between devices, on_device(): lax.all_gather(master.astype(jnp.bfloat16), 'dp', axis=0, tiled=True)  17.5 us
    unnamed x40, local copies, waits for them, and re-layouts  16.1 us
    dot_general x1, matrix products, on_device(): lax.dot_general(spike_cols, grad_flat, (((0,), (0,)), ((), ())), preferre...  10.2 us
    unnamed x12, other arithmetic  9.82 us
  transfers between devices with their start and end apart: 7, of which 4 were waited for; matrix products, arithmetic and copies ran while one was open for 29% of the time, Pallas kernels for 0%

commit v1 on v0

--- a/solution.py
+++ b/solution.py
@@ -75,7 +75,7 @@
     data_count = lax.axis_size("dp")
     total_cells = samples * data_count * lax.axis_size("rep") * rows * lax.axis_size("space") * cols
     shard_part = lax.psum_scatter(weight_local, "dp", scatter_dimension=0, tiled=True)
-    summed = lax.psum(shard_part, ("space", "rep"))
+    summed = jnp.sum(lax.all_gather(shard_part, ("space", "rep")), axis=0)
     weight_grad = summed * (1.0 / math.sqrt(steps_count * total_cells))
     new_moment = 0.9 * moment + 0.1 * weight_grad
     new_second = 0.95 * second + 0.05 * weight_grad * weight_grad

time: 353 us -> 417 us (1.18)
  waiting for transfers between devices: 212 us -> 271 us
  other arithmetic: 32.3 us -> 39.8 us
    all_gather x0 -> x1, waiting for transfers between devices: none -> 64.8 us  [on_device(): summed = jnp.sum(lax.all_gather(shard_part, ('space', 'rep')), axis=0)]
    psum x1 -> x0, waiting for transfers between devices: 61.5 us -> none  [on_device(): summed = lax.psum(shard_part, ('space', 'rep'))]
    reduce_scatter x1, waiting for transfers between devices: 132 us -> 165 us  [on_device(): lax.psum_scatter(weight_local, 'dp', scatter_dimension=0, tiled=True)]
    all_gather x1, waiting for transfers between devices: 17.5 us -> 39.2 us  [on_device(): lax.all_gather(master.astype(jnp.bfloat16), 'dp', axis=0, tiled=True)]
    reduce_sum x0 -> x1, other arithmetic: none -> 10.4 us  [on_device(): summed = jnp.sum(lax.all_gather(shard_part, ('space', 'rep')), axis=0)]
    unnamed x40 -> x34, local copies, waits for them, and re-layouts: 16.1 us -> 16 us
  transfers between devices with their start and end apart: 7 -> 7, of which waited for: 4 -> 5; matrix products, arithmetic and copies ran while one was open for 29% -> 20% of each run, Pallas kernels for 0% -> 0%
where the time goes in v1:
time: 417 us; the launch traced here: 416 us
  waiting for transfers between devices  271 us (65%)
  local copies, waits for them, and re-layouts  46.1 us (11%)
  other arithmetic  39.8 us (10%)
  matrix products  35.9 us (9%)
  between operations  14 us (3%)
  starting transfers between devices  8.97 us (2%)
    reduce_scatter x1, waiting for transfers between devices, on_device(): lax.psum_scatter(weight_local, 'dp', scatter_dimension=0, tiled=True)  165 us
    all_gather x1, waiting for transfers between devices, on_device(): summed = jnp.sum(lax.all_gather(shard_part, ('space', 'rep')), axis=0)  64.8 us
    all_gather x1, waiting for transfers between devices, on_device(): lax.all_gather(master.astype(jnp.bfloat16), 'dp', axis=0, tiled=True)  39.2 us
    reshape x1, local copies, waits for them, and re-layouts, on_device(): grad_cols = jnp.concatenate([grad_pad[:, :, 1 - a:1 - a + rows, 1 - b:1 -...  26.6 us
    dot_general x1, matrix products, on_device(): jnp.einsum('nkd,kcd->nc', grad_cols, weights.reshape(9, chans, chans), pr...  25.8 us
    unnamed x34, local copies, waits for them, and re-layouts  16 us
    reduce_sum x1, other arithmetic, on_device(): summed = jnp.sum(lax.all_gather(shard_part, ('space', 'rep')), axis=0)  10.4 us
    dot_general x1, matrix products, on_device(): lax.dot_general(spike_cols, grad_flat, (((0,), (0,)), ((), ())), preferre...  10.1 us
  transfers between devices with their start and end apart: 7, of which 5 were waited for; matrix products, arithmetic and copies ran while one was open for 20% of the time, Pallas kernels for 0%

profile of v1, /device:TPU:0, one launch (start us, length us, event | category | flops | bytes accessed | tf_op | source)
XLA Modules:
  0.0 415.8 jit_solution(10228255993633196208)
XLA Ops:
  7.2 1.2 pad_maximum_fusion.4
  8.4 1.3 collective-permute-start.3
  9.7 3.0 collective-permute-start.2
  12.8 1.1 collective-permute-done.2
  21.3 10.1 %fusion.4 = f32[4608,512]{1,0:T(8,128)} fusion(bf16[6,1,8,32,4608]{4,3,2,0,1:T(8,128)(2,1)S(1)} %fusion.21, bf16[6,1,8,32,512]{4,3,2,1,0:T(8,128)(2,1)S(1)} %copy-done), kind=kOutput, calls=%fused_computation.4 | convolution fusion | flops 7247757312 | bytes 25165824 | tf_op jit(solution)/shard_map/dot_general | solution.py:58
  31.5 2.8 convert_element_type.357
  34.4 165.0 %reduce-scatter.2.cloned.1.call-done = f32[1152,512]{1,0:T(8,128)} async-done(((f32[4608,512]{1,0:T(8,128)}), f32[1152,512]{1,0:T(8,128)}) %reduce-scatter.2.cloned.1.call-update) | async-done | bytes 2359312 | tf_op jit(solution)/shard_map/reduce_scatter | solution.py:77
  199.5 1.1 fusion.104
  200.5 1.3 collective-permute-start.1
  201.8 3.2 collective-permute-start
  205.9 2.3 fusion.15
  208.2 1.7 slice_dynamic-update-slice_fusion.8
  210.0 1.5 fusion.23
  211.5 1.4 slice_dynamic-update-slice_fusion.7
  212.9 2.0 slice_dynamic-update-slice_fusion.6
  214.9 1.4 constant_dynamic-update-slice_fusion
  216.3 1.5 slice_dynamic-update-slice_fusion.5
  217.8 2.0 slice_dynamic-update-slice_fusion.4
  219.8 1.4 fusion.22
  221.2 1.4 slice_dynamic-update-slice_fusion.3
  222.6 26.6 %reshape.515 = bf16[1536,9,512]{2,1,0:T(8,128)(2,1)} reshape(bf16[6,1,8,32,4608]{4,3,2,1,0:T(8,128)(2,1)} %slice_dynamic-update-slice_fusion.3) | data formatting | bytes 28311552 | tf_op jit(solution)/shard_map/reshape | solution.py:56
  249.2 0.9 fusion.73
  250.2 0.9 convert_bitcast_fusion.1
  251.1 1.6 fusion.28
  252.7 39.2 %all-gather.4.cloned.1.call-done = bf16[4608,512]{1,0:T(8,128)(2,1)} async-done(((bf16[1152,512]{1,0:T(8,128)(2,1)}), bf16[4608,512]{1,0:T(8,128)(2,1)}) %all-gather.4.cloned.1.call-update) | async-done | bytes 4718608 | tf_op jit(solution)/shard_map/all_gather | solution.py:31
  291.9 25.8 %fusion.8 = f32[1536,512]{1,0:T(8,128)S(1)} fusion(bf16[9,512,512]{2,1,0:T(8,128)(2,1)} %bitcast.160, bf16[1536,9,512]{2,1,0:T(8,128)(2,1)} %reshape.515), kind=kOutput, calls=%fused_computation.8 | convolution fusion | flops 7247757312 | bytes 22020096 | tf_op jit(solution)/shard_map/nkd,kcd->nc/dot_general | solution.py:61
  319.6 1.7 broadcast_multiply_fusion.1
  322.1 0.9 fusion.87
  324.5 0.9 fusion.93
  326.2 64.8 %all-gather.6.cloned.1.call-done = f32[9216,512]{1,0:T(8,128)} async-done(((f32[1152,512]{1,0:T(8,128)}), f32[9216,512]{1,0:T(8,128)}) %all-gather.6.cloned.1.call-update) | async-done | bytes 18874384 | tf_op jit(solution)/shard_map/all_gather | solution.py:78
  391.0 10.4 %reduce_sum.9 = f32[1152,512]{1,0:T(8,128)} reduce(f32[8,1152,512]{2,1,0:T(8,128)} %bitcast.149, f32[]{:T(128)} %constant.28.clone.1), dimensions={0}, to_apply=%region_1.2 | reduce | flops 4128768 | bytes 21233668 | tf_op jit(solution)/shard_map/reduce_sum | solution.py:78
  401.4 7.9 %add_divide_fusion = (f32[1152,512]{1,0:T(8,128)}, f32[1152,512]{1,0:T(8,128)}, f32[1152,512]{1,0:T(8,128)}, f32[1152,512]{1,0:T(8,128)}) fusion(f32[1152,512]{1,0:T(8,128)} %reduce_sum.9, f32[1152,512]{1,0:T(8,128)} %param.11, f32[1152,512]{1,0:T(8,128)} %param.10), kind=kLoop, calls=%fused_computation.14 | loop fusion | flops 5898240 | bytes 16515072 | tf_op jit(solution)/shard_map/div | solution.py:82
  (50 shorter events, 13.3 us)
Async XLA Ops:
  7.2 6.7 %copy-start.9 = (bf16[1,8,32,512]{3,2,1,0:T(8,128)(2,1)S(1)}, bf16[1,8,32,512]{3,2,1,0:T(8,128)(2,1)}, u32[]{:S(2)}) copy-start(bf16[1,8,32,512]{3,2,1,0:T(8,128)(2,1)} %param.7) | copy-start | bytes 786436
  7.2 192.3 %reduce-scatter.2.cloned.1.call-start = ((), (), s32[]{:S(2)}) async-start(), calls=%async_computation.2 | async-start | bytes 11796480 | tf_op jit(solution)/shard_map/reduce_scatter | solution.py:77
  7.2 6.6 %copy-start.3 = (bf16[6,1,8,32,512]{4,3,2,1,0:T(8,128)(2,1)S(1)}, bf16[6,1,8,32,512]{4,3,2,1,0:T(8,128)(2,1)}, u32[]{:S(2)}) copy-start(bf16[6,1,8,32,512]{4,3,2,1,0:T(8,128)(2,1)} %param.6) | copy-start | bytes 4718596
  8.4 4.4 %collective-permute-start.3 = (bf16[7,1,1,32,512]{4,3,2,1,0:T(8,128)(2,1)S(1)}, bf16[7,1,1,32,512]{4,3,2,1,0:T(8,128)(2,1)S(1)}, u32[]{:S(2)}, u32[]{:S(2)}) collective-permute-start(bf16[7,1,1,32,512]{4,3,2,1,0:T(8,128)(2,1)S(1)} %get-tuple-element.28), channel_id=1, source_target_pairs={{2,0},{4,2},{6,4},{3,1},{5,3},{7,5},{10,8},{12,10},{14,12},{11,9},... | collective-permute-start | bytes 688136 | tf_op jit(solution)/shard_map/ppermute | solution.py:16
  9.7 4.1 collective-permute-start.2
  19.9 1.4 copy-start
  31.5 260.4 %all-gather.4.cloned.1.call-start = ((), (), s32[]{:S(2)}) async-start(), calls=%async_computation.1 | async-start | bytes 5898240 | tf_op jit(solution)/shard_map/all_gather | solution.py:31
  34.4 356.6 %all-gather.6.cloned.1.call-start = ((), (), s32[]{:S(2)}) async-start(), calls=%async_computation.3 | async-start | bytes 21233664 | tf_op jit(solution)/shard_map/all_gather | solution.py:78
  200.5 4.5 %collective-permute-start.1 = (bf16[6,1,1,32,512]{4,3,2,1,0:T(8,128)(2,1)S(1)}, bf16[6,1,1,32,512]{4,3,2,1,0:T(8,128)(2,1)S(1)}, u32[]{:S(2)}, u32[]{:S(2)}) collective-permute-start(bf16[6,1,1,32,512]{4,3,2,1,0:T(8,128)(2,1)S(1)} %get-tuple-element.30), channel_id=1, source_target_pairs={{2,0},{4,2},{6,4},{3,1},{5,3},{7,5},{10,8},{12,10},{14,12},{11,9},... | collective-permute-start | bytes 589832 | tf_op jit(solution)/shard_map/ppermute | solution.py:16
  201.8 4.1 collective-permute-start
  208.2 1.8 copy-start.1
  317.7 1.1 copy-start.4
  317.7 1.3 copy-start.5
  317.7 1.5 copy-start.6
  317.7 1.7 copy-start.7
  317.7 1.8 copy-start.8
  319.5 1.7 copy-start.2
Sparse Core Ops, SparseCore 0:
  31.6 167.7 reduce-scatter.1
  201.6 90.2 all-gather.3
  293.7 97.1 all-gather.5
